TPU v7x, 256 devices: a whole 4x4x8 slice. The times are simulated.
256 devices in a mesh: row: 32 (over z, x), col: 8 (over y, core).
Axes of the slice: x: 4, y: 4, z: 8, core: 2. Of those that a mesh axis runs over, the one named last changes fastest.
Arguments:
- x_points: bfloat16 [32768, 64], P(('row', 'col')), may hold values from -6 to 6
- y_points: bfloat16 [65536, 64], P(('col', 'row')), may hold values from -6 to 6
- row_mass: bfloat16 [32768], P(('row', 'col')), may hold values from 1 to 30, as said below
- col_mass: bfloat16 [65536], P(('col', 'row')), may hold values from 1 to 30, as said below
- multipliers: bfloat16 [32768, 64], P(('row', 'col')), may hold values from -12 to 12
- col_potential: bfloat16 [65536], P(('col', 'row')), may hold values from -3 to 3
- basket: float32 [64], replicated, may hold values from 0.05 to 0.25
- damping: float32 [64], replicated, may hold values from 0.3 to 1.5
Outputs:
- row_potential: float32 [32768], P('row')
- col_potential_new: float32 [65536], P('col')
- multipliers_new: float32 [32768, 64], P(('row', 'col'))
Inputs may be any that keep to these rules, and one draw needn't show every extreme that they name: `row_mass`: weights rise along the points' order by up to a factor of three. `col_mass`: weights rise along the points' order by up to a factor of three.
All inputs are finite; a program needn't handle non-finite values.
Results may differ from a plain program's by a relative error of at most 0.0012.
Values may be sent and summed in bfloat16 or wider, within the bound.
No kernel may reach another device: no remote copies, remote signals or barrier semaphores. Data moves between devices by JAX's collectives and lax.ppermute only.
A program may use at most 64 MiB of HBM per device.

v0:
```python
import jax
import jax.numpy as jnp
from jax import lax
from jax.sharding import PartitionSpec as P

EPS = 0.5
KAPPA = 0.5
RIDGE = 1.0


def joined(value, axis, join):
    pieces = jax.tree.map(lambda part: lax.all_gather(part, axis), value)
    head = jax.tree.map(lambda part: part[0], pieces)
    tail = jax.tree.map(lambda part: part[1:], pieces)
    subtotal, _ = lax.scan(lambda subtotal, piece: (join(subtotal, piece), None), head, tail)
    return subtotal


def prepare_rows(x_rows, mult_rows, basket):
    xf = x_rows.astype(jnp.float32)
    hf = mult_rows.astype(jnp.float32)
    width = xf.shape[1]
    query = hf + 2.0 * KAPPA / width * xf
    row_term = -jnp.sum(hf * xf, axis=1) - KAPPA / width * jnp.sum(xf * xf, axis=1)
    row_basket = jnp.sum(xf * basket[None, :], axis=1)
    return (query, row_term, row_basket)


def prepare_cols(y_cols, basket):
    yf = y_cols.astype(jnp.float32)
    width = yf.shape[1]
    col_term = -(KAPPA / width) * jnp.sum(yf * yf, axis=1)
    col_basket = jnp.sum(yf * basket[None, :], axis=1)
    features = jnp.concatenate([yf, yf * yf], axis=1).astype(jnp.bfloat16)
    return (yf, col_term, col_basket, features)


def scores(query, row_term, row_basket, y_float, col_term, col_basket):
    dots = lax.dot_general(
        query,
        y_float,
        (((1,), (1,)), ((), ())),
        precision=lax.Precision.HIGHEST,
        preferred_element_type=jnp.float32,
    )
    payoff = jax.nn.relu(col_basket[None, :] - row_basket[:, None])
    return (dots + row_term[:, None] + col_term[None, :] + payoff) / EPS


def lse_join(first, second):
    top = jnp.maximum(first[0], second[0])
    total = first[1] * jnp.exp(first[0] - top) + second[1] * jnp.exp(second[0] - top)
    return (top, total)


def on_device(x_points, y_points, row_mass, col_mass, multipliers, col_potential, basket, damping):
    x_rows, mult_rows, mass_rows = (
        lax.all_gather(x_points, "col", axis=0, tiled=True),
        lax.all_gather(multipliers, "col", axis=0, tiled=True),
        lax.all_gather(row_mass, "col", axis=0, tiled=True),
    )
    y_cols, pot_cols, mass_cols = (
        lax.all_gather(y_points, "row", axis=0, tiled=True),
        lax.all_gather(col_potential, "row", axis=0, tiled=True),
        lax.all_gather(col_mass, "row", axis=0, tiled=True),
    )
    query, row_term, row_basket = prepare_rows(x_rows, mult_rows, basket)
    y_float, col_term, col_basket, features = prepare_cols(y_cols, basket)
    row_weight = mass_rows.astype(jnp.float32)
    col_weight = mass_cols.astype(jnp.float32)
    log_row = jnp.log(row_weight)
    log_col = jnp.log(col_weight)
    nrows = x_rows.shape[0]
    block = min(128, nrows)
    count = nrows // block
    starts = jnp.arange(count, dtype=jnp.int32) * block

    def cut(arr, start):
        return lax.dynamic_slice_in_dim(arr, start, block, 0)

    def block_scores(start):
        return scores(
            cut(query, start),
            cut(row_term, start),
            cut(row_basket, start),
            y_float,
            col_term,
            col_basket,
        )

    gshift = pot_cols.astype(jnp.float32) / EPS + log_col

    def row_pass(start):
        z = block_scores(start) + gshift[None, :]
        top = jnp.max(z, axis=1)
        total = jnp.sum(jnp.exp(z - top[:, None]), axis=1)
        return (top, total)

    row_tops, row_totals = lax.map(row_pass, starts)
    row_tops = row_tops.reshape(nrows)
    row_totals = row_totals.reshape(nrows)
    mu_total, nu_total = lax.psum(
        (jnp.sum(row_mass.astype(jnp.float32)), jnp.sum(col_mass.astype(jnp.float32))),
        ("row", "col"),
    )
    row_top, row_total = joined((row_tops, row_totals), "col", lse_join)
    log_nu_total = jnp.log(nu_total)
    row_potential = -EPS * (row_top + jnp.log(row_total) - log_nu_total)
    fshift = row_potential / EPS + log_row

    def col_pass(start):
        z = block_scores(start) + cut(fshift, start)[:, None]
        top = jnp.max(z, axis=0)
        total = jnp.sum(jnp.exp(z - top[None, :]), axis=0)
        return (top, total)

    col_tops, col_totals = lax.map(col_pass, starts)
    col_top = jnp.max(col_tops, axis=0)
    col_total = jnp.sum(col_totals * jnp.exp(col_tops - col_top[None, :]), axis=0)
    peak = lax.pmax(col_top, "row")
    scaled = col_total * jnp.exp(col_top - peak)
    whole = lax.psum(scaled, "row")
    col_potential_new = -EPS * (peak + jnp.log(whole) - jnp.log(mu_total))
    gq = col_potential_new / EPS + log_col - log_nu_total
    fq = row_potential / EPS

    def moment_pass(start):
        plan = jnp.exp(block_scores(start) + cut(fq, start)[:, None] + gq[None, :]).astype(
            jnp.bfloat16
        )
        both = jnp.dot(plan, features, preferred_element_type=jnp.float32)
        mass = jnp.sum(plan.astype(jnp.float32), axis=1)
        return (both, mass)

    both, mass = lax.map(moment_pass, starts)
    both = both.reshape(nrows, features.shape[1])
    mass = mass.reshape(nrows)
    share = x_points.shape[0]
    both_all, mass_all = lax.psum((both, mass), "col")
    offset = lax.axis_index("col") * share
    own_both = lax.dynamic_slice_in_dim(both_all, offset, share, 0)
    own_mass = lax.dynamic_slice_in_dim(mass_all, offset, share, 0)
    width = x_points.shape[1]
    first = own_both[:, :width]
    second = own_both[:, width:]
    xf = x_points.astype(jnp.float32)
    grad = first - xf * own_mass[:, None]
    curv = (second - 2.0 * xf * first + xf * xf * own_mass[:, None]) / EPS + RIDGE
    multipliers_new = multipliers.astype(jnp.float32) - damping[None, :] * grad / curv
    return (row_potential, col_potential_new, multipliers_new)


def solution(mesh):
    placed = (
        P(("row", "col"), None),
        P(("col", "row"), None),
        P(("row", "col")),
        P(("col", "row")),
        P(("row", "col"), None),
        P(("col", "row")),
        P(),
        P(),
    )
    return jax.shard_map(
        on_device,
        mesh=mesh,
        in_specs=placed,
        out_specs=(P("row"), P("col"), P(("row", "col"), None)),
        check_vma=False,
    )
```

profile of v0, /device:TPU:2, one launch (start us, length us, event | category | flops | bytes accessed | tf_op | source)
XLA Modules:
  0.0 851.1 jit_solution(13461661143674850518)
XLA Ops:
  7.2 1.5 copy.17
  8.8 1.3 convert_reduce_fusion.1
  10.0 1.3 convert_reduce_fusion.2
  11.3 79.4 %all-reduce = (f32[]{:T(128)}, f32[]{:T(128)}) all-reduce(f32[]{:T(128)} %convert_reduce_fusion.1, f32[]{:T(128)} %convert_reduce_fusion.2), channel_id=1, replica_groups=mesh['row'=32,'col'=8] {'row','col'}, use_global_device_ids=true, to_apply=%region_12.13 | all-reduce | flops 2 | bytes 16 | tf_op jit(solution)/shard_map/psum | solution.py:102
  95.0 42.6 %all-gather.1 = bf16[32,1,256]{2,1,0:T(2,128)(2,1)S(1)} all-gather(bf16[1,1,256]{2,1,0:T(2,128)(2,1)S(1)} %reshape.38), channel_id=1, replica_groups=mesh['row'=32,'col'=8] {'row'}, dimensions={0}, use_global_device_ids=true | all-gather | bytes 16896 | tf_op jit(solution)/shard_map/all_gather | solution.py:65
  137.6 40.5 %all-gather = bf16[32,1,256]{2,1,0:T(2,128)(2,1)S(1)} all-gather(bf16[1,1,256]{2,1,0:T(2,128)(2,1)S(1)} %reshape.36), channel_id=1, replica_groups=mesh['row'=32,'col'=8] {'row'}, dimensions={0}, use_global_device_ids=true | all-gather | bytes 16896 | tf_op jit(solution)/shard_map/all_gather | solution.py:64
  178.2 9.2 %all-gather.4 = bf16[8,1,128]{2,1,0:T(2,128)(2,1)S(1)} all-gather(bf16[1,1,128]{2,1,0:T(2,128)(2,1)} %bitcast.86), channel_id=1, replica_groups=mesh['row'=32,'col'=8] {'col'}, dimensions={0}, use_global_device_ids=true | all-gather | bytes 2304 | tf_op jit(solution)/shard_map/all_gather | solution.py:60
  187.4 12.8 %all_gather.24 = bf16[1024,64]{1,0:T(8,128)(2,1)S(1)} all-gather(bf16[128,64]{1,0:T(8,128)(2,1)S(1)} %copy.15), channel_id=1, replica_groups=mesh['row'=32,'col'=8] {'col'}, dimensions={0}, use_global_device_ids=true | all-gather | bytes 147456 | tf_op jit(solution)/shard_map/all_gather | solution.py:59
  200.2 12.8 %all_gather.25 = bf16[1024,64]{1,0:T(8,128)(2,1)S(1)} all-gather(bf16[128,64]{1,0:T(8,128)(2,1)S(1)} %copy.16), channel_id=1, replica_groups=mesh['row'=32,'col'=8] {'col'}, dimensions={0}, use_global_device_ids=true | all-gather | bytes 147456 | tf_op jit(solution)/shard_map/all_gather | solution.py:58
  213.1 1.2 fusion.24
  214.3 5.2 multiply_reduce_fusion
  219.5 2.2 convert_element_type.39
  221.7 80.0 %while.48 = (s32[]{:T(128)}, f32[8,128]{1,0:T(8,128)S(1)}, f32[8,128]{1,0:T(8,128)S(1)}, s32[8]{0:T(128)S(1)}, f32[1024,64]{1,0:T(8,128)S(1)}, /*index=5*/f32[81...) while((s32[]{:T(128)}, f32[8,128]{1,0:T(8,128)S(1)}, ...), condition=%wide.region_8.9_spmd, body=%wide.region_5.8_spmd.sunk | while | flops 815791872 | bytes 10656463 | solution.py:99
  224.4 6.5 fusion.52
  234.4 6.5 fusion.52
  244.4 6.5 fusion.52
  254.4 6.5 fusion.52
  264.4 6.5 fusion.52
  274.4 6.5 fusion.52
  284.4 6.5 fusion.52
  294.4 6.5 fusion.52
  301.7 12.9 %all-gather.2 = f32[8,1,1024]{2,1,0:T(1,128)S(1)} all-gather(f32[1,1,1024]{2,1,0:T(1,128)S(1)} %bitcast.83), channel_id=1, replica_groups=mesh['row'=32,'col'=8] {'col'}, dimensions={0}, use_global_device_ids=true | all-gather | bytes 36864 | tf_op jit(solution)/shard_map/all_gather | solution.py:12
  314.7 13.1 %all-gather.3 = f32[8,1,1024]{2,1,0:T(1,128)S(1)} all-gather(f32[1,1,1024]{2,1,0:T(1,128)S(1)} %bitcast.82), channel_id=1, replica_groups=mesh['row'=32,'col'=8] {'col'}, dimensions={0}, use_global_device_ids=true | all-gather | bytes 36864 | tf_op jit(solution)/shard_map/all_gather | solution.py:12
  328.7 80.8 %while.50 = (s32[]{:T(128)}, f32[8,8192]{1,0:T(8,128)S(1)}, f32[8,8192]{1,0:T(8,128)S(1)}, s32[8]{0:T(128)S(1)}, f32[1024,64]{1,0:T(8,128)S(1)}, /*index=5*/f32[...) while((s32[]{:T(128)}, f32[8,8192]{1,0:T(8,128)S(1)}, ...), condition=%wide.region_16.17_spmd, body=%wide.region_13.16_spmd.sunk | while | flops 815775744 | bytes 10851027 | solution.py:117
  331.5 6.4 fusion.54
  341.6 6.4 fusion.54
  351.7 6.4 fusion.54
  361.8 6.4 fusion.54
  371.9 6.4 fusion.54
  382.0 6.4 fusion.54
  392.1 6.4 fusion.54
  402.2 6.4 fusion.54
  409.7 136.0 %pmax.7 = f32[8192]{0:T(1024)S(1)} all-reduce(f32[8192]{0:T(1024)S(1)} %reduce_max.27), channel_id=1, replica_groups=mesh['row'=32,'col'=8] {'row'}, use_global_device_ids=true, to_apply=%region_18.19 | all-reduce | flops 8192 | bytes 65536 | tf_op jit(solution)/shard_map/pmax | solution.py:120
  545.8 139.9 %psum.36 = f32[8192]{0:T(1024)S(1)} all-reduce(f32[8192]{0:T(1024)S(1)} %exponential_multiply_fusion), channel_id=1, replica_groups=mesh['row'=32,'col'=8] {'row'}, use_global_device_ids=true, to_apply=%region_20.21 | all-reduce | flops 8192 | bytes 65536 | tf_op jit(solution)/shard_map/psum | solution.py:122
  686.4 3.4 pad_maximum_fusion
  689.8 88.4 %while.51 = (s32[]{:T(128)}, f32[8,128,128]{2,1,0:T(8,128)S(1)}, f32[8,128]{1,0:T(8,128)S(1)}, s32[8]{0:T(128)S(1)}, f32[1024,64]{1,0:T(8,128)S(1)}, /*index=5*/...) while((s32[]{:T(128)}, f32[8,128,128]{2,1,0:T(8,128)S(1)}, ...), condition=%wide.region_25.26_spmd, body=%wide.region_23.25_spmd.sunk | while | flops 1085276032 | bytes 8624355 | solution.py:135
  692.5 7.5 convert_reduce_fusion.4
  703.6 7.5 convert_reduce_fusion.4
  714.6 7.5 convert_reduce_fusion.4
  725.7 7.5 convert_reduce_fusion.4
  736.7 7.5 convert_reduce_fusion.4
  747.8 7.5 convert_reduce_fusion.4
  758.8 7.5 convert_reduce_fusion.4
  769.9 7.5 convert_reduce_fusion.4
  778.1 1.0 copy.19
  779.2 12.4 %psum.39 = f32[1024]{0:T(1024)S(1)} all-reduce(f32[1024]{0:T(1024)S(1)} %bitcast.84), channel_id=1, replica_groups=mesh['row'=32,'col'=8] {'col'}, use_global_device_ids=true, to_apply=%region_27.28 | all-reduce | flops 1024 | bytes 8192 | tf_op jit(solution)/shard_map/psum | solution.py:139
  791.7 51.1 %all-reduce.3.cloned.1.call-done = f32[1024,128]{0,1:T(8,128)} async-done(((f32[1024,128]{0,1:T(8,128)}), f32[1024,128]{0,1:T(8,128)}) %all-reduce.3.cloned.1.call-update) | async-done | bytes 524304 | tf_op jit(solution)/shard_map/psum | solution.py:139
  842.8 1.5 fusion.28
  (209 shorter events, 44.4 us)
Async XLA Ops:
  7.2 207.1 %all-gather.7.cloned.1.call-start = ((), (), s32[]{:S(2)}) async-start(), calls=%async_computation | async-start | bytes 2162688 | tf_op jit(solution)/shard_map/all_gather | solution.py:63
  8.7 834.1 %all-reduce.3.cloned.1.call-start = ((), (), s32[]{:S(2)}) async-start(), calls=%async_computation.1 | async-start | bytes 1048576 | tf_op jit(solution)/shard_map/psum | solution.py:139
  214.3 5.2 copy-start
  689.7 153.1 %copy-start.1 = (bf16[128,64]{0,1:T(8,128)(2,1)S(1)}, bf16[128,64]{0,1:T(8,128)(2,1)}, u32[]{:S(2)}) copy-start(bf16[128,64]{0,1:T(8,128)(2,1)} %param.16) | copy-start | bytes 49156
  689.7 153.1 %copy-start.2 = (bf16[128,64]{0,1:T(8,128)(2,1)S(1)}, bf16[128,64]{0,1:T(8,128)(2,1)}, u32[]{:S(2)}) copy-start(bf16[128,64]{0,1:T(8,128)(2,1)} %param.20) | copy-start | bytes 49156
  689.8 153.1 %copy-start.3 = (f32[64]{0:T(128)S(1)}, f32[64]{0:T(128)}, u32[]{:S(2)}) copy-start(f32[64]{0:T(128)} %param.23) | copy-start | bytes 772
Sparse Core Ops, SparseCore 0:
  10.6 79.5 all-gather.6
  779.3 63.4 all-reduce.2
where the time goes:
time: 853 us; the launch traced here: 851 us
  blocking collectives  512 us (60%)
  matrix products  169 us (20%)
  waiting for transfers between devices  51.2 us (6%)
  loops' own time  47.5 us (6%)
  other arithmetic  28.6 us (3%)
  local copies, waits for them, and re-layouts  27.8 us (3%)
  between operations  15.6 us (2%)
    dot_general x24, matrix products, scores(): lax.dot_general(query, y_float, (((1,), (1,)), ((), ())), precision=lax.P...  163 us
    psum x1, blocking collectives, on_device(): whole = lax.psum(scaled, 'row')  140 us
    pmax x1, blocking collectives, on_device(): peak = lax.pmax(col_top, 'row')  136 us
    psum x1, blocking collectives, on_device(): lax.psum((jnp.sum(row_mass.astype(jnp.float32)), jnp.sum(col_mass.astype(...  79.4 us
    psum x1, waiting for transfers between devices, on_device(): both_all, mass_all = lax.psum((both, mass), 'col')  51.1 us
    all_gather x1, blocking collectives, on_device(): lax.all_gather(col_mass, 'row', axis=0, tiled=True)  42.6 us
    all_gather x1, blocking collectives, on_device(): lax.all_gather(col_potential, 'row', axis=0, tiled=True)  40.5 us
    all_gather x2, blocking collectives, joined(): pieces = jax.tree.map(lambda part: lax.all_gather(part, axis), value)  26 us
  transfers between devices with their start and end apart: 2, of which 1 were waited for; matrix products, arithmetic and copies ran while one was open for 1% of the time, Pallas kernels for 0%

commit v1 on v0

--- a/solution.py
+++ b/solution.py
@@ -61,7 +61,9 @@
     )
     y_cols, pot_cols, mass_cols = (
         lax.all_gather(y_points, "row", axis=0, tiled=True),
-        lax.all_gather(col_potential, "row", axis=0, tiled=True),
+        jnp.concatenate(
+            lax.all_to_all(jnp.stack([col_potential] * lax.axis_size("row")), "row", 0, 0), axis=0
+        ),
         lax.all_gather(col_mass, "row", axis=0, tiled=True),
     )
     query, row_term, row_basket = prepare_rows(x_rows, mult_rows, basket)

time: 853 us -> 823 us (0.965)
  blocking collectives: 512 us -> 468 us
  starting transfers between devices: 0.08 us -> 11.7 us
    all_gather x1 -> x0, blocking collectives: 40.5 us -> none  [on_device(): lax.all_gather(col_potential, 'row', axis=0, tiled=True)]
    all_to_all x0 -> x1, starting transfers between devices: none -> 11.6 us  [on_device(): lax.all_to_all(jnp.stack([col_potential] * lax.axis_size('row')), 'row',...]
  transfers between devices with their start and end apart: 2 -> 3, of which waited for: 1 -> 1; matrix products, arithmetic and copies ran while one was open for 1% -> 1% of each run, Pallas kernels for 0% -> 0%
where the time goes in v1:
time: 823 us; the launch traced here: 821 us
  blocking collectives  468 us (57%)
  matrix products  168 us (20%)
  waiting for transfers between devices  51.9 us (6%)
  loops' own time  47.5 us (6%)
  other arithmetic  29.3 us (4%)
  local copies, waits for them, and re-layouts  29 us (4%)
  between operations  15.6 us (2%)
  starting transfers between devices  11.7 us (1%)
    dot_general x24, matrix products, scores(): lax.dot_general(query, y_float, (((1,), (1,)), ((), ())), precision=lax.P...  163 us
    psum x1, blocking collectives, on_device(): whole = lax.psum(scaled, 'row')  140 us
    pmax x1, blocking collectives, on_device(): peak = lax.pmax(col_top, 'row')  136 us
    psum x1, blocking collectives, on_device(): lax.psum((jnp.sum(row_mass.astype(jnp.float32)), jnp.sum(col_mass.astype(...  75 us
    psum x1, waiting for transfers between devices, on_device(): both_all, mass_all = lax.psum((both, mass), 'col')  51.9 us
    all_gather x1, blocking collectives, on_device(): lax.all_gather(col_mass, 'row', axis=0, tiled=True)  42.4 us
    all_gather x2, blocking collectives, joined(): pieces = jax.tree.map(lambda part: lax.all_gather(part, axis), value)  26 us
  transfers between devices with their start and end apart: 3, of which 1 were waited for; matrix products, arithmetic and copies ran while one was open for 1% of the time, Pallas kernels for 0%

profile of v1, /device:TPU:2, one launch (start us, length us, event | category | flops | bytes accessed | tf_op | source)
XLA Modules:
  0.0 821.4 jit_solution(8236116233020089111)
XLA Ops:
  7.2 1.5 copy.17
  11.3 11.6 %all-to-all-start = ((bf16[32,2,128]{2,1,0:T(2,128)(2,1)}), bf16[32,2,128]{2,1,0:T(2,128)(2,1)S(1)}, u32[]{:S(2)}, u32[]{:S(2)}) async-start(bf16[32,2,128]{2,1,0:T(2,128)(2,1)} %reshape.68), calls=%async_computation | async-start | bytes 32768 | tf_op jit(solution)/shard_map/all_to_all | solution.py:65
  25.3 11.0 %all-gather.3 = bf16[8,1,128]{2,1,0:T(2,128)(2,1)S(1)} all-gather(bf16[1,1,128]{2,1,0:T(2,128)(2,1)} %bitcast.86), channel_id=1, replica_groups=mesh['row'=32,'col'=8] {'col'}, dimensions={0}, use_global_device_ids=true | all-gather | bytes 2304 | tf_op jit(solution)/shard_map/all_gather | solution.py:60
  36.2 42.4 %all-gather = bf16[32,1,256]{2,1,0:T(2,128)(2,1)S(1)} all-gather(bf16[1,1,256]{2,1,0:T(2,128)(2,1)S(1)} %reshape.48), channel_id=1, replica_groups=mesh['row'=32,'col'=8] {'row'}, dimensions={0}, use_global_device_ids=true | all-gather | bytes 16896 | tf_op jit(solution)/shard_map/all_gather | solution.py:67
  78.7 12.8 %all_gather.21 = bf16[1024,64]{1,0:T(8,128)(2,1)S(1)} all-gather(bf16[128,64]{1,0:T(8,128)(2,1)S(1)} %copy.15), channel_id=1, replica_groups=mesh['row'=32,'col'=8] {'col'}, dimensions={0}, use_global_device_ids=true | all-gather | bytes 147456 | tf_op jit(solution)/shard_map/all_gather | solution.py:59
  91.5 12.8 %all_gather.22 = bf16[1024,64]{1,0:T(8,128)(2,1)S(1)} all-gather(bf16[128,64]{1,0:T(8,128)(2,1)S(1)} %copy.16), channel_id=1, replica_groups=mesh['row'=32,'col'=8] {'col'}, dimensions={0}, use_global_device_ids=true | all-gather | bytes 147456 | tf_op jit(solution)/shard_map/all_gather | solution.py:58
  104.3 1.3 convert_reduce_fusion.1
  105.6 1.3 convert_reduce_fusion.2
  106.8 1.2 fusion.24
  108.1 75.0 %all-reduce = (f32[]{:T(128)}, f32[]{:T(128)}) all-reduce(f32[]{:T(128)} %convert_reduce_fusion.1, f32[]{:T(128)} %convert_reduce_fusion.2), channel_id=1, replica_groups=mesh['row'=32,'col'=8] {'row','col'}, use_global_device_ids=true, to_apply=%region_12.13 | all-reduce | flops 2 | bytes 16 | tf_op jit(solution)/shard_map/psum | solution.py:104
  184.6 5.2 multiply_reduce_fusion
  189.8 2.2 convert_element_type.40
  192.0 79.9 %while.48 = (s32[]{:T(128)}, f32[8,128]{1,0:T(8,128)S(1)}, f32[8,128]{1,0:T(8,128)S(1)}, s32[8]{0:T(128)S(1)}, f32[1024,64]{1,0:T(8,128)S(1)}, /*index=5*/f32[81...) while((s32[]{:T(128)}, f32[8,128]{1,0:T(8,128)S(1)}, ...), condition=%wide.region_8.9_spmd, body=%wide.region_5.8_spmd.sunk | while | flops 815791872 | bytes 10656463 | solution.py:101
  194.7 6.5 fusion.52
  204.7 6.5 fusion.52
  214.7 6.5 fusion.52
  224.7 6.5 fusion.52
  234.7 6.5 fusion.52
  244.7 6.5 fusion.52
  254.7 6.5 fusion.52
  264.7 6.5 fusion.52
  272.0 12.9 %all-gather.1 = f32[8,1,1024]{2,1,0:T(1,128)S(1)} all-gather(f32[1,1,1024]{2,1,0:T(1,128)S(1)} %bitcast.83), channel_id=1, replica_groups=mesh['row'=32,'col'=8] {'col'}, dimensions={0}, use_global_device_ids=true | all-gather | bytes 36864 | tf_op jit(solution)/shard_map/all_gather | solution.py:12
  284.9 13.1 %all-gather.2 = f32[8,1,1024]{2,1,0:T(1,128)S(1)} all-gather(f32[1,1,1024]{2,1,0:T(1,128)S(1)} %bitcast.82), channel_id=1, replica_groups=mesh['row'=32,'col'=8] {'col'}, dimensions={0}, use_global_device_ids=true | all-gather | bytes 36864 | tf_op jit(solution)/shard_map/all_gather | solution.py:12
  299.0 80.8 %while.50 = (s32[]{:T(128)}, f32[8,8192]{1,0:T(8,128)S(1)}, f32[8,8192]{1,0:T(8,128)S(1)}, s32[8]{0:T(128)S(1)}, f32[1024,64]{1,0:T(8,128)S(1)}, /*index=5*/f32[...) while((s32[]{:T(128)}, f32[8,8192]{1,0:T(8,128)S(1)}, ...), condition=%wide.region_16.17_spmd, body=%wide.region_13.16_spmd.sunk | while | flops 815775744 | bytes 10851027 | solution.py:119
  301.8 6.4 fusion.54
  311.9 6.4 fusion.54
  322.0 6.4 fusion.54
  332.1 6.4 fusion.54
  342.2 6.4 fusion.54
  352.3 6.4 fusion.54
  362.4 6.4 fusion.54
  372.5 6.4 fusion.54
  379.9 135.7 %pmax.7 = f32[8192]{0:T(1024)S(1)} all-reduce(f32[8192]{0:T(1024)S(1)} %reduce_max.27), channel_id=1, replica_groups=mesh['row'=32,'col'=8] {'row'}, use_global_device_ids=true, to_apply=%region_18.19 | all-reduce | flops 8192 | bytes 65536 | tf_op jit(solution)/shard_map/pmax | solution.py:122
  515.7 139.9 %psum.36 = f32[8192]{0:T(1024)S(1)} all-reduce(f32[8192]{0:T(1024)S(1)} %exponential_multiply_fusion), channel_id=1, replica_groups=mesh['row'=32,'col'=8] {'row'}, use_global_device_ids=true, to_apply=%region_20.21 | all-reduce | flops 8192 | bytes 65536 | tf_op jit(solution)/shard_map/psum | solution.py:124
  656.3 3.4 pad_maximum_fusion
  659.7 87.9 %while.51 = (s32[]{:T(128)}, f32[8,128,128]{2,1,0:T(8,128)S(1)}, f32[8,128]{1,0:T(8,128)S(1)}, s32[8]{0:T(128)S(1)}, f32[1024,64]{1,0:T(8,128)S(1)}, /*index=5*/...) while((s32[]{:T(128)}, f32[8,128,128]{2,1,0:T(8,128)S(1)}, ...), condition=%wide.region_25.26_spmd, body=%wide.region_23.25_spmd.sunk | while | flops 1085276032 | bytes 8624355 | solution.py:137
  662.5 7.5 convert_reduce_fusion.4
  673.5 7.5 convert_reduce_fusion.4
  684.5 7.5 convert_reduce_fusion.4
  695.4 7.5 convert_reduce_fusion.4
  706.4 7.5 convert_reduce_fusion.4
  717.4 7.5 convert_reduce_fusion.4
  728.4 7.5 convert_reduce_fusion.4
  739.4 7.5 convert_reduce_fusion.4
  747.6 1.0 copy.19
  748.6 12.4 %psum.39 = f32[1024]{0:T(1024)S(1)} all-reduce(f32[1024]{0:T(1024)S(1)} %bitcast.84), channel_id=1, replica_groups=mesh['row'=32,'col'=8] {'col'}, use_global_device_ids=true, to_apply=%region_27.28 | all-reduce | flops 1024 | bytes 8192 | tf_op jit(solution)/shard_map/psum | solution.py:141
  761.1 51.9 %all-reduce.3.cloned.1.call-done = f32[1024,128]{0,1:T(8,128)} async-done(((f32[1024,128]{0,1:T(8,128)}), f32[1024,128]{0,1:T(8,128)}) %all-reduce.3.cloned.1.call-update) | async-done | bytes 524304 | tf_op jit(solution)/shard_map/psum | solution.py:141
  813.0 1.5 fusion.28
  (214 shorter events, 46.0 us)
Async XLA Ops:
  7.2 177.5 %all-gather.6.cloned.1.call-start = ((), (), s32[]{:S(2)}) async-start(), calls=%async_computation.1 | async-start | bytes 2162688 | tf_op jit(solution)/shard_map/all_gather | solution.py:63
  11.3 173.3 %all-to-all-start = ((bf16[32,2,128]{2,1,0:T(2,128)(2,1)}), bf16[32,2,128]{2,1,0:T(2,128)(2,1)S(1)}, u32[]{:S(2)}, u32[]{:S(2)}) async-start(bf16[32,2,128]{2,1,0:T(2,128)(2,1)} %reshape.68), calls=%async_computation | async-start | bytes 32768 | tf_op jit(solution)/shard_map/all_to_all | solution.py:65
  22.9 790.2 %all-reduce.3.cloned.1.call-start = ((), (), s32[]{:S(2)}) async-start(), calls=%async_computation.2 | async-start | bytes 1048576 | tf_op jit(solution)/shard_map/psum | solution.py:141
  184.6 5.2 copy-start
  659.7 153.4 %copy-start.1 = (bf16[128,64]{0,1:T(8,128)(2,1)S(1)}, bf16[128,64]{0,1:T(8,128)(2,1)}, u32[]{:S(2)}) copy-start(bf16[128,64]{0,1:T(8,128)(2,1)} %param.16) | copy-start | bytes 49156
  659.7 153.4 %copy-start.2 = (bf16[128,64]{0,1:T(8,128)(2,1)S(1)}, bf16[128,64]{0,1:T(8,128)(2,1)}, u32[]{:S(2)}) copy-start(bf16[128,64]{0,1:T(8,128)(2,1)} %param.20) | copy-start | bytes 49156
  659.7 153.3 %copy-start.3 = (f32[64]{0:T(128)S(1)}, f32[64]{0:T(128)}, u32[]{:S(2)}) copy-start(f32[64]{0:T(128)} %param.23) | copy-start | bytes 772
Sparse Core Ops, SparseCore 0:
  10.6 79.6 all-gather.5
  748.8 64.2 all-reduce.2
